TPU v7x, 32 devices: a whole 2x2x4 slice. The times are simulated.
32 devices in a mesh: row: 4 (over y, x), col: 8 (over z, core).
Axes of the slice: x: 2, y: 2, z: 4, core: 2. Of those that a mesh axis runs over, the one named last changes fastest.
Arguments:
- frames: bfloat16 [4096, 440], P('col'), may hold values from -6 to 6
- center_picks: int32 [8, 8, 64], P('col'), may hold values from 0 to 511, as said below
- send_counts: int32 [8, 8], P(None, 'col'), may hold values from 0 to 64, as said below
- send_offsets: int32 [8, 8], P(None, 'col'), may hold values from 0 to 256, as said below
Outputs:
- factor_panels: float32 [4, 512, 1024], P('row', 'col')
- trailing: float32 [4, 512, 8, 256], P('row', None, 'col')
Inputs may be any that keep to these rules, and one draw needn't show every extreme that they name: `center_picks`: for each owner the entries over all destinations and slots are distinct local frame indices. `send_counts`: for each destination the counts over owners sum to 256; every destination has an owner that fills all 64 slots and one that sends nothing. `send_offsets`: for each destination the owners' segments [offset, offset + count) cover 0 to 255 without intersection, in an order that varies by destination; an owner that sends nothing may start at 256.
All inputs are finite; a program needn't handle non-finite values.
Results may differ from a plain program's by a relative error of at most 0.0003.
Values may be sent and summed in bfloat16 or wider, within the bound.
No kernel may reach another device: no remote copies, remote signals or barrier semaphores. Data moves between devices by JAX's collectives and lax.ppermute only.
A program may use at most 128 MiB of HBM per device.

v0:
```python
import jax
import jax.numpy as jnp
from jax import lax
from jax.sharding import PartitionSpec as P

PANEL = 256
PANELS = 4
CENT_DEV = 256
kernel_scale = 0.6
ridge_shift = 0.1


def spread(value, axis, source):
    kept = jnp.where(lax.axis_index(axis) == source, value, 0).astype(value.dtype)
    return lax.psum(kept, axis)


def gaussian(left_feats, right_feats):
    inner = lax.dot_general(
        left_feats, right_feats, (((1,), (1,)), ((), ())), preferred_element_type=jnp.float32
    )
    left_norm = jnp.sum(jnp.square(left_feats.astype(jnp.float32)), axis=1)
    right_norm = jnp.sum(jnp.square(right_feats.astype(jnp.float32)), axis=1)
    feat_width = left_feats.shape[1]
    return jnp.exp(
        -(kernel_scale / feat_width) * (left_norm[:, None] + right_norm[None, :] - 2.0 * inner)
    )


def outer_minus(column, panel_cols, rows_piece):
    return column - lax.dot_general(
        panel_cols,
        rows_piece,
        (((1,), (1,)), ((), ())),
        precision=lax.Precision.HIGHEST,
        preferred_element_type=jnp.float32,
    )


def make_panel(column, factor, row_tile, panel_step):
    solved = jax.scipy.linalg.solve_triangular(factor, column.T, lower=True).T
    repeated = jnp.tile(factor, (column.shape[0] // factor.shape[0], 1))
    return jnp.where(
        (row_tile > panel_step)[:, None],
        solved,
        jnp.where((row_tile == panel_step)[:, None], repeated, jnp.zeros_like(solved)),
    )


def update_slots(columns, panel_cols, col_rows):
    columns[0] = outer_minus(columns[0], panel_cols, col_rows)
    return columns


def per_device(frames, center_picks, send_counts, send_offsets):
    rows_axis = lax.axis_size("row")
    cols_axis = lax.axis_size("col")
    row_id = lax.axis_index("row")
    col_id = lax.axis_index("col")
    feat_width = frames.shape[1]
    capacity = center_picks.shape[2]
    outgoing = frames[center_picks[0]]
    incoming = lax.all_to_all(outgoing, "col", split_axis=0, concat_axis=0, tiled=True)
    position = jnp.arange(CENT_DEV, dtype=jnp.int32)
    starts = send_offsets[:, 0]
    lengths = send_counts[:, 0]
    inside = (position[:, None] >= starts[None, :]) & (
        position[:, None] < (starts + lengths)[None, :]
    )
    source = jnp.sum(jnp.where(inside, jnp.arange(cols_axis, dtype=jnp.int32)[None, :], 0), axis=1)
    within = position - jnp.sum(jnp.where(inside, starts[None, :], 0), axis=1)
    own_feats = incoming.reshape(cols_axis * capacity, feat_width)[source * capacity + within]
    col_slots = CENT_DEV // PANEL
    row_tiles_dev = col_slots * cols_axis // rows_axis
    rows_dev = row_tiles_dev * PANEL
    tile_range = jnp.arange(row_tiles_dev, dtype=jnp.int32)
    gathered = lax.all_gather(own_feats, "col", axis=0, tiled=True)
    blocks = gathered.reshape(cols_axis, col_slots, PANEL, feat_width)
    my_tiles = row_id + rows_axis * tile_range
    row_feats = blocks[my_tiles % cols_axis, my_tiles // cols_axis].reshape(rows_dev, feat_width)
    local_rows = jnp.arange(rows_dev, dtype=jnp.int32)
    row_tile = row_id + rows_axis * (local_rows // PANEL)
    global_row = row_tile * PANEL + local_rows % PANEL
    local_cols = jnp.arange(CENT_DEV, dtype=jnp.int32)
    global_col = (col_id + cols_axis * (local_cols // PANEL)) * PANEL + local_cols % PANEL
    kernel = gaussian(row_feats, own_feats) + ridge_shift * (
        global_row[:, None] == global_col[None, :]
    ).astype(jnp.float32)
    columns = [kernel]
    panels = []
    for panel_step in range(PANELS):
        slot_now = panel_step // cols_axis
        tile_slot = panel_step // rows_axis
        diag_here = columns[slot_now][tile_slot * PANEL : (tile_slot + 1) * PANEL]
        diag_block = spread(diag_here, "row", panel_step % rows_axis)
        factor = jnp.linalg.cholesky(diag_block)
        panel_here = make_panel(columns[slot_now], factor, row_tile, panel_step)
        panel_cols = spread(panel_here, "col", panel_step % cols_axis)
        here_rows = lax.dynamic_slice_in_dim(
            panel_cols, (col_id + 0) // rows_axis * PANEL, PANEL, 0
        )
        col_rows = spread(here_rows, "row", col_id % rows_axis)
        panels.append(panel_cols)
        columns = update_slots(columns, panel_cols, col_rows)
    trailing = columns[0].reshape(1, rows_dev, 1, CENT_DEV)
    every_panel = jnp.concatenate(panels, axis=1)
    share_rows = rows_dev // cols_axis
    panel_share = lax.dynamic_slice_in_dim(every_panel, col_id * share_rows, share_rows, 0).reshape(
        1, share_rows, PANELS * PANEL
    )
    return (panel_share, trailing)


def solution(mesh):
    in_specs = (P("col", None), P("col", None, None), P(None, "col"), P(None, "col"))
    out_specs = (P("row", "col", None), P("row", None, "col", None))
    return jax.shard_map(
        per_device, mesh=mesh, in_specs=in_specs, out_specs=out_specs, check_vma=False
    )
```

profile of v0, /device:TPU:0, one launch (start us, length us, event | category | flops | bytes accessed | tf_op | source)
XLA Modules:
  0.0 926.6 jit_solution(15417714206202597751)
XLA Ops:
  11.8 6.3 all-to-all-start
  18.3 15.2 %all-to-all-done = bf16[8,64,440]{2,1,0:T(8,128)(2,1)S(1)} async-done(((bf16[8,64,440]{2,1,0:T(8,128)(2,1)}), bf16[8,64,440]{2,1,0:T(8,128)(2,1)S(1)}, u32[]{:S(2)}, u32[]{:S(2)}) %all-to-all-start) | async-done | bytes 450592 | tf_op jit(solution)/shard_map/all_to_all | solution.py:63
  36.6 27.0 %all-gather.3.cloned.1.call-done = bf16[2048,440]{1,0:T(8,128)(2,1)} async-done(((bf16[256,440]{1,0:T(8,128)(2,1)}), bf16[2048,440]{1,0:T(8,128)(2,1)}) %all-gather.3.cloned.1.call-update) | async-done | bytes 1802256 | tf_op jit(solution)/shard_map/all_gather | solution.py:77
  67.6 42.3 %all-reduce.14.cloned.1.call-done = f32[256,256]{0,1:T(8,128)} async-done(((f32[256,256]{0,1:T(8,128)}), f32[256,256]{0,1:T(8,128)}) %all-reduce.14.cloned.1.call-update) | async-done | bytes 262160 | tf_op jit(solution)/shard_map/psum | solution.py:15
  112.0 11.7 %cholesky.214 = f32[128,128]{1,0:T(8,128)S(1)} custom-call(f32[128,128]{1,0:T(8,128)S(1)} %cholesky.346), custom_call_target="Cholesky" | custom-call | tf_op jit(solution)/shard_map/jit(cholesky)/cholesky | solution.py:96
  123.7 9.8 %custom-call.19 = f32[1,128,128]{1,2,0:T(8,128)S(1)} custom-call(f32[1,128,128]{2,1,0:T(8,128)S(1)} %get-tuple-element.105), custom_call_target="InvertDiagBlocksLowerTriangular" | custom-call | tf_op jit(solution)/shard_map/jit(cholesky)/cholesky | solution.py:96
  134.0 11.7 %cholesky.231 = f32[128,128]{1,0:T(8,128)S(1)} custom-call(f32[128,128]{1,0:T(8,128)S(1)} %convolution_subtract_fusion.8), custom_call_target="Cholesky" | custom-call | tf_op jit(solution)/shard_map/jit(cholesky)/cholesky | solution.py:96
  148.0 4.6 while.8
  152.6 19.7 %custom-call.20 = f32[2,128,128]{1,2,0:T(8,128)S(1)} custom-call(f32[2,128,128]{2,1,0:T(8,128)S(1)} %get-tuple-element.30), custom_call_target="InvertDiagBlocksLowerTriangular" | custom-call | tf_op jit(solution)/shard_map/jit(_solve_triangular)/triangular_solve | solution.py:41
  174.8 56.2 %all-reduce.16.cloned.1.call-done = f32[512,256]{0,1:T(8,128)} async-done(((f32[512,256]{0,1:T(8,128)}), f32[512,256]{0,1:T(8,128)}) %all-reduce.16.cloned.1.call-update) | async-done | bytes 524304 | tf_op jit(solution)/shard_map/psum | solution.py:15
  232.8 43.5 %all-reduce.18.cloned.1.call-done = f32[256,256]{0,1:T(8,128)} async-done(((f32[256,256]{0,1:T(8,128)}), f32[256,256]{0,1:T(8,128)}) %all-reduce.18.cloned.1.call-update) | async-done | bytes 262160 | tf_op jit(solution)/shard_map/psum | solution.py:15
  279.2 43.7 %all-reduce.20.cloned.1.call-done = f32[256,256]{0,1:T(8,128)} async-done(((f32[256,256]{0,1:T(8,128)}), f32[256,256]{0,1:T(8,128)}) %all-reduce.20.cloned.1.call-update) | async-done | bytes 262160 | tf_op jit(solution)/shard_map/psum | solution.py:15
  325.0 11.7 %cholesky.248 = f32[128,128]{1,0:T(8,128)S(1)} custom-call(f32[128,128]{1,0:T(8,128)S(1)} %cholesky.349), custom_call_target="Cholesky" | custom-call | tf_op jit(solution)/shard_map/jit(cholesky)/cholesky | solution.py:96
  336.8 9.8 %custom-call.21 = f32[1,128,128]{1,2,0:T(8,128)S(1)} custom-call(f32[1,128,128]{2,1,0:T(8,128)S(1)} %get-tuple-element.101), custom_call_target="InvertDiagBlocksLowerTriangular" | custom-call | tf_op jit(solution)/shard_map/jit(cholesky)/cholesky | solution.py:96
  347.1 11.7 %cholesky.265 = f32[128,128]{1,0:T(8,128)S(1)} custom-call(f32[128,128]{1,0:T(8,128)S(1)} %convolution_subtract_fusion.7), custom_call_target="Cholesky" | custom-call | tf_op jit(solution)/shard_map/jit(cholesky)/cholesky | solution.py:96
  365.9 19.7 %custom-call.22 = f32[2,128,128]{1,2,0:T(8,128)S(1)} custom-call(f32[2,128,128]{2,1,0:T(8,128)S(1)} %get-tuple-element.31), custom_call_target="InvertDiagBlocksLowerTriangular" | custom-call | tf_op jit(solution)/shard_map/jit(_solve_triangular)/triangular_solve | solution.py:41
  388.1 56.3 %all-reduce.22.cloned.1.call-done = f32[512,256]{0,1:T(8,128)} async-done(((f32[512,256]{0,1:T(8,128)}), f32[512,256]{0,1:T(8,128)}) %all-reduce.22.cloned.1.call-update) | async-done | bytes 524304 | tf_op jit(solution)/shard_map/psum | solution.py:15
  446.2 43.9 %all-reduce.24.cloned.1.call-done = f32[256,256]{0,1:T(8,128)} async-done(((f32[256,256]{0,1:T(8,128)}), f32[256,256]{0,1:T(8,128)}) %all-reduce.24.cloned.1.call-update) | async-done | bytes 262160 | tf_op jit(solution)/shard_map/psum | solution.py:15
  492.8 43.8 %all-reduce.26.cloned.1.call-done = f32[256,256]{0,1:T(8,128)} async-done(((f32[256,256]{0,1:T(8,128)}), f32[256,256]{0,1:T(8,128)}) %all-reduce.26.cloned.1.call-update) | async-done | bytes 262160 | tf_op jit(solution)/shard_map/psum | solution.py:15
  538.6 11.7 %cholesky.282 = f32[128,128]{1,0:T(8,128)S(1)} custom-call(f32[128,128]{1,0:T(8,128)S(1)} %cholesky.352), custom_call_target="Cholesky" | custom-call | tf_op jit(solution)/shard_map/jit(cholesky)/cholesky | solution.py:96
  550.4 9.8 %custom-call.23 = f32[1,128,128]{1,2,0:T(8,128)S(1)} custom-call(f32[1,128,128]{2,1,0:T(8,128)S(1)} %get-tuple-element.97), custom_call_target="InvertDiagBlocksLowerTriangular" | custom-call | tf_op jit(solution)/shard_map/jit(cholesky)/cholesky | solution.py:96
  560.7 11.7 %cholesky.299 = f32[128,128]{1,0:T(8,128)S(1)} custom-call(f32[128,128]{1,0:T(8,128)S(1)} %convolution_subtract_fusion.6), custom_call_target="Cholesky" | custom-call | tf_op jit(solution)/shard_map/jit(cholesky)/cholesky | solution.py:96
  579.5 19.7 %custom-call.24 = f32[2,128,128]{1,2,0:T(8,128)S(1)} custom-call(f32[2,128,128]{2,1,0:T(8,128)S(1)} %get-tuple-element.32), custom_call_target="InvertDiagBlocksLowerTriangular" | custom-call | tf_op jit(solution)/shard_map/jit(_solve_triangular)/triangular_solve | solution.py:41
  601.8 56.3 %all-reduce.28.cloned.1.call-done = f32[512,256]{0,1:T(8,128)} async-done(((f32[512,256]{0,1:T(8,128)}), f32[512,256]{0,1:T(8,128)}) %all-reduce.28.cloned.1.call-update) | async-done | bytes 524304 | tf_op jit(solution)/shard_map/psum | solution.py:15
  659.8 43.5 %all-reduce.30.cloned.1.call-done = f32[256,256]{0,1:T(8,128)} async-done(((f32[256,256]{0,1:T(8,128)}), f32[256,256]{0,1:T(8,128)}) %all-reduce.30.cloned.1.call-update) | async-done | bytes 262160 | tf_op jit(solution)/shard_map/psum | solution.py:15
  706.0 44.0 %all-reduce.32.cloned.1.call-done = f32[256,256]{0,1:T(8,128)} async-done(((f32[256,256]{0,1:T(8,128)}), f32[256,256]{0,1:T(8,128)}) %all-reduce.32.cloned.1.call-update) | async-done | bytes 262160 | tf_op jit(solution)/shard_map/psum | solution.py:15
  752.1 11.7 %cholesky.316 = f32[128,128]{1,0:T(8,128)S(1)} custom-call(f32[128,128]{1,0:T(8,128)S(1)} %cholesky.355), custom_call_target="Cholesky" | custom-call | tf_op jit(solution)/shard_map/jit(cholesky)/cholesky | solution.py:96
  763.9 9.8 %custom-call.25 = f32[1,128,128]{1,2,0:T(8,128)S(1)} custom-call(f32[1,128,128]{2,1,0:T(8,128)S(1)} %get-tuple-element.93), custom_call_target="InvertDiagBlocksLowerTriangular" | custom-call | tf_op jit(solution)/shard_map/jit(cholesky)/cholesky | solution.py:96
  774.2 11.7 %cholesky.333 = f32[128,128]{1,0:T(8,128)S(1)} custom-call(f32[128,128]{1,0:T(8,128)S(1)} %convolution_subtract_fusion.5), custom_call_target="Cholesky" | custom-call | tf_op jit(solution)/shard_map/jit(cholesky)/cholesky | solution.py:96
  792.8 19.7 %custom-call.26 = f32[2,128,128]{1,2,0:T(8,128)S(1)} custom-call(f32[2,128,128]{2,1,0:T(8,128)S(1)} %get-tuple-element.33), custom_call_target="InvertDiagBlocksLowerTriangular" | custom-call | tf_op jit(solution)/shard_map/jit(_solve_triangular)/triangular_solve | solution.py:41
  815.1 56.3 %all-reduce.34.cloned.1.call-done = f32[512,256]{0,1:T(8,128)} async-done(((f32[512,256]{0,1:T(8,128)}), f32[512,256]{0,1:T(8,128)}) %all-reduce.34.cloned.1.call-update) | async-done | bytes 524304 | tf_op jit(solution)/shard_map/psum | solution.py:15
  875.1 41.9 %all-reduce.36.cloned.1.call-done = f32[256,256]{0,1:T(8,128)} async-done(((f32[256,256]{0,1:T(8,128)}), f32[256,256]{0,1:T(8,128)}) %all-reduce.36.cloned.1.call-update) | async-done | bytes 262160 | tf_op jit(solution)/shard_map/psum | solution.py:15
  (186 shorter events, 85.8 us)
Async XLA Ops:
  9.2 9.0 copy-start.5
  9.2 9.0 copy-start.6
  11.8 21.7 %all-to-all-start = ((bf16[8,64,440]{2,1,0:T(8,128)(2,1)}), bf16[8,64,440]{2,1,0:T(8,128)(2,1)S(1)}, u32[]{:S(2)}, u32[]{:S(2)}) async-start(bf16[8,64,440]{2,1,0:T(8,128)(2,1)} %bitcast.1), calls=%async_computation | async-start | bytes 1048576 | tf_op jit(solution)/shard_map/all_to_all | solution.py:63
  18.1 45.4 %all-gather.3.cloned.1.call-start = ((), (), s32[]{:S(2)}) async-start(), calls=%async_computation.13 | async-start | bytes 2359296 | tf_op jit(solution)/shard_map/all_gather | solution.py:77
  35.3 30.6 %copy-start.4 = (bf16[256,440]{1,0:T(8,128)(2,1)S(1)}, bf16[256,440]{1,0:T(8,128)(2,1)}, u32[]{:S(2)}) copy-start(bf16[256,440]{1,0:T(8,128)(2,1)} %gather_fusion.1) | copy-start | bytes 675844
  35.4 74.5 %all-reduce.14.cloned.1.call-start = ((), (), s32[]{:S(2)}) async-start(), calls=%async_computation.1 | async-start | bytes 524288 | tf_op jit(solution)/shard_map/psum | solution.py:15
  67.3 163.8 %all-reduce.16.cloned.1.call-start = ((), (), s32[]{:S(2)}) async-start(), calls=%async_computation.2 | async-start | bytes 1048576 | tf_op jit(solution)/shard_map/psum | solution.py:15
  174.8 101.6 %all-reduce.18.cloned.1.call-start = ((), (), s32[]{:S(2)}) async-start(), calls=%async_computation.3 | async-start | bytes 524288 | tf_op jit(solution)/shard_map/psum | solution.py:15
  232.8 90.2 %all-reduce.20.cloned.1.call-start = ((), (), s32[]{:S(2)}) async-start(), calls=%async_computation.4 | async-start | bytes 524288 | tf_op jit(solution)/shard_map/psum | solution.py:15
  279.1 165.3 %all-reduce.22.cloned.1.call-start = ((), (), s32[]{:S(2)}) async-start(), calls=%async_computation.5 | async-start | bytes 1048576 | tf_op jit(solution)/shard_map/psum | solution.py:15
  388.1 102.0 %all-reduce.24.cloned.1.call-start = ((), (), s32[]{:S(2)}) async-start(), calls=%async_computation.6 | async-start | bytes 524288 | tf_op jit(solution)/shard_map/psum | solution.py:15
  446.1 90.5 %all-reduce.26.cloned.1.call-start = ((), (), s32[]{:S(2)}) async-start(), calls=%async_computation.7 | async-start | bytes 524288 | tf_op jit(solution)/shard_map/psum | solution.py:15
  492.7 165.4 %all-reduce.28.cloned.1.call-start = ((), (), s32[]{:S(2)}) async-start(), calls=%async_computation.8 | async-start | bytes 1048576 | tf_op jit(solution)/shard_map/psum | solution.py:15
  601.7 101.6 %all-reduce.30.cloned.1.call-start = ((), (), s32[]{:S(2)}) async-start(), calls=%async_computation.9 | async-start | bytes 524288 | tf_op jit(solution)/shard_map/psum | solution.py:15
  659.8 90.3 %all-reduce.32.cloned.1.call-start = ((), (), s32[]{:S(2)}) async-start(), calls=%async_computation.10 | async-start | bytes 524288 | tf_op jit(solution)/shard_map/psum | solution.py:15
  706.0 165.4 %all-reduce.34.cloned.1.call-start = ((), (), s32[]{:S(2)}) async-start(), calls=%async_computation.11 | async-start | bytes 1048576 | tf_op jit(solution)/shard_map/psum | solution.py:15
  814.0 59.1 %copy-start.1 = (f32[512,256]{0,1:T(8,128)S(1)}, f32[512,256]{0,1:T(8,128)}, u32[]{:S(2)}) copy-start(f32[512,256]{0,1:T(8,128)} %all-reduce.16.cloned.1.call-done) | copy-start | bytes 1572868
  814.0 59.1 %copy-start.2 = (f32[512,256]{0,1:T(8,128)S(1)}, f32[512,256]{0,1:T(8,128)}, u32[]{:S(2)}) copy-start(f32[512,256]{0,1:T(8,128)} %all-reduce.22.cloned.1.call-done) | copy-start | bytes 1572868
  814.0 59.1 %copy-start.3 = (f32[512,256]{0,1:T(8,128)S(1)}, f32[512,256]{0,1:T(8,128)}, u32[]{:S(2)}) copy-start(f32[512,256]{0,1:T(8,128)} %all-reduce.28.cloned.1.call-done) | copy-start | bytes 1572868
  815.0 102.0 %all-reduce.36.cloned.1.call-start = ((), (), s32[]{:S(2)}) async-start(), calls=%async_computation.12 | async-start | bytes 524288 | tf_op jit(solution)/shard_map/psum | solution.py:15
  871.3 45.7 %copy-start = (f32[512,256]{0,1:T(8,128)S(1)}, f32[512,256]{0,1:T(8,128)}, u32[]{:S(2)}) copy-start(f32[512,256]{0,1:T(8,128)} %all-reduce.34.cloned.1.call-done) | copy-start | bytes 1572868
Sparse Core Ops, SparseCore 0:
  35.5 27.9 all-gather.2
  67.4 42.4 all-reduce.13
  174.9 56.1 all-reduce.15
  234.4 41.8 all-reduce.17
  280.0 42.9 all-reduce.19
  388.2 56.1 all-reduce.21
  448.2 41.8 all-reduce.23
  493.6 42.9 all-reduce.25
  601.9 56.1 all-reduce.27
  661.4 41.9 all-reduce.29
  707.1 42.9 all-reduce.31
  815.1 56.1 all-reduce.33
  875.1 41.8 all-reduce.35
where the time goes:
time: 930 us; the launch traced here: 927 us
  waiting for transfers between devices  614 us (66%)
  other arithmetic  238 us (26%)
  local copies, waits for them, and re-layouts  31.9 us (3%)
  between operations  20.4 us (2%)
  matrix products  14 us (2%)
    psum x12, waiting for transfers between devices, spread(): return lax.psum(kept, axis)  572 us
    another operation x27, other arithmetic, per_device(): factor = jnp.linalg.cholesky(diag_block)  138 us
    another operation x9, other arithmetic, make_panel(): solved = jax.scipy.linalg.solve_triangular(factor, column.T, lower=True).T  78.8 us
    all_gather x1, waiting for transfers between devices, per_device(): gathered = lax.all_gather(own_feats, 'col', axis=0, tiled=True)  27 us
  transfers between devices with their start and end apart: 14, of which 14 were waited for; matrix products, arithmetic and copies ran while one was open for 0% of the time, Pallas kernels for 0%

commit v1 on v0

--- a/solution.py
+++ b/solution.py
@@ -10,9 +10,15 @@
 ridge_shift = 0.1
 
 
+def gather_and_add(block, axis):
+    pieces = lax.all_gather(block, axis, axis=0, tiled=False)
+    total = pieces.sum(axis=0)
+    return total
+
+
 def spread(value, axis, source):
     kept = jnp.where(lax.axis_index(axis) == source, value, 0).astype(value.dtype)
-    return lax.psum(kept, axis)
+    return gather_and_add(kept, axis)
 
 
 def gaussian(left_feats, right_feats):

time: 930 us -> 761 us (0.82)
  waiting for transfers between devices: 614 us -> 438 us
  other arithmetic: 238 us -> 253 us
    psum x12 -> x0, waiting for transfers between devices: 572 us -> none  [spread(): return lax.psum(kept, axis)]
    all_gather x0 -> x12, waiting for transfers between devices: none -> 396 us  [gather_and_add(): pieces = lax.all_gather(block, axis, axis=0, tiled=False)]
    reduce_sum x0 -> x12, other arithmetic: none -> 20.6 us  [gather_and_add(): total = pieces.sum(axis=0)]
where the time goes in v1:
time: 761 us; the launch traced here: 758 us
  waiting for transfers between devices  438 us (58%)
  other arithmetic  253 us (33%)
  local copies, waits for them, and re-layouts  26.7 us (4%)
  between operations  20.2 us (3%)
  matrix products  11 us (1%)
    all_gather x12, waiting for transfers between devices, gather_and_add(): pieces = lax.all_gather(block, axis, axis=0, tiled=False)  396 us
    another operation x27, other arithmetic, per_device(): factor = jnp.linalg.cholesky(diag_block)  138 us
    another operation x9, other arithmetic, make_panel(): solved = jax.scipy.linalg.solve_triangular(factor, column.T, lower=True).T  79.6 us
    all_gather x1, waiting for transfers between devices, per_device(): gathered = lax.all_gather(own_feats, 'col', axis=0, tiled=True)  27 us
    reduce_sum x12, other arithmetic, gather_and_add(): total = pieces.sum(axis=0)  20.6 us
    another operation x33, local copies, waits for them, and re-layouts, make_panel(): solved = jax.scipy.linalg.solve_triangular(factor, column.T, lower=True).T  16.8 us
  transfers between devices with their start and end apart: 14, of which 14 were waited for; matrix products, arithmetic and copies ran while one was open for 0% of the time, Pallas kernels for 0%

profile of v1, /device:TPU:0, one launch (start us, length us, event | category | flops | bytes accessed | tf_op | source)
XLA Modules:
  0.0 757.6 jit_solution(11719426082781270576)
XLA Ops:
  11.8 6.3 all-to-all-start
  18.3 15.2 %all-to-all-done = bf16[8,64,440]{2,1,0:T(8,128)(2,1)S(1)} async-done(((bf16[8,64,440]{2,1,0:T(8,128)(2,1)}), bf16[8,64,440]{2,1,0:T(8,128)(2,1)S(1)}, u32[]{:S(2)}, u32[]{:S(2)}) %all-to-all-start) | async-done | bytes 450592 | tf_op jit(solution)/shard_map/all_to_all | solution.py:69
  36.6 27.0 %all-gather.27.cloned.1.call-done = bf16[2048,440]{1,0:T(8,128)(2,1)} async-done(((bf16[256,440]{1,0:T(8,128)(2,1)}), bf16[2048,440]{1,0:T(8,128)(2,1)}) %all-gather.27.cloned.1.call-update) | async-done | bytes 1802256 | tf_op jit(solution)/shard_map/all_gather | solution.py:83
  67.6 25.9 %all-gather.29.cloned.1.call-done = f32[1024,256]{1,0:T(8,128)} async-done(((f32[256,256]{1,0:T(8,128)}), f32[1024,256]{1,0:T(8,128)}) %all-gather.29.cloned.1.call-update) | async-done | bytes 1048592 | tf_op jit(solution)/shard_map/all_gather | solution.py:14
  95.1 11.7 %cholesky.214 = f32[128,128]{1,0:T(8,128)S(1)} custom-call(f32[128,128]{1,0:T(8,128)S(1)} %cholesky.346), custom_call_target="Cholesky" | custom-call | tf_op jit(solution)/shard_map/jit(cholesky)/cholesky | solution.py:102
  106.8 9.8 %custom-call.19 = f32[1,128,128]{1,2,0:T(8,128)S(1)} custom-call(f32[1,128,128]{2,1,0:T(8,128)S(1)} %get-tuple-element.107), custom_call_target="InvertDiagBlocksLowerTriangular" | custom-call | tf_op jit(solution)/shard_map/jit(cholesky)/cholesky | solution.py:102
  117.1 11.7 %cholesky.231 = f32[128,128]{1,0:T(8,128)S(1)} custom-call(f32[128,128]{1,0:T(8,128)S(1)} %convolution_subtract_fusion.8), custom_call_target="Cholesky" | custom-call | tf_op jit(solution)/shard_map/jit(cholesky)/cholesky | solution.py:102
  131.1 4.7 while.8
  135.8 19.7 %custom-call.20 = f32[2,128,128]{1,2,0:T(8,128)S(1)} custom-call(f32[2,128,128]{2,1,0:T(8,128)S(1)} %get-tuple-element.30), custom_call_target="InvertDiagBlocksLowerTriangular" | custom-call | tf_op jit(solution)/shard_map/jit(_solve_triangular)/triangular_solve | solution.py:47
  158.1 47.2 %all-gather.31.cloned.1.call-done = f32[4096,256]{1,0:T(8,128)} async-done(((f32[512,256]{1,0:T(8,128)}), f32[4096,256]{1,0:T(8,128)}) %all-gather.31.cloned.1.call-update) | async-done | bytes 4194320 | tf_op jit(solution)/shard_map/all_gather | solution.py:14
  208.6 25.4 %all-gather.33.cloned.1.call-done = f32[1024,256]{1,0:T(8,128)} async-done(((f32[256,256]{1,0:T(8,128)}), f32[1024,256]{1,0:T(8,128)}) %all-gather.33.cloned.1.call-update) | async-done | bytes 1048592 | tf_op jit(solution)/shard_map/all_gather | solution.py:14
  237.1 26.7 %all-gather.35.cloned.1.call-done = f32[1024,256]{1,0:T(8,128)} async-done(((f32[256,256]{1,0:T(8,128)}), f32[1024,256]{1,0:T(8,128)}) %all-gather.35.cloned.1.call-update) | async-done | bytes 1048592 | tf_op jit(solution)/shard_map/all_gather | solution.py:14
  265.3 11.7 %cholesky.248 = f32[128,128]{1,0:T(8,128)S(1)} custom-call(f32[128,128]{1,0:T(8,128)S(1)} %cholesky.349), custom_call_target="Cholesky" | custom-call | tf_op jit(solution)/shard_map/jit(cholesky)/cholesky | solution.py:102
  277.1 9.8 %custom-call.21 = f32[1,128,128]{1,2,0:T(8,128)S(1)} custom-call(f32[1,128,128]{2,1,0:T(8,128)S(1)} %get-tuple-element.103), custom_call_target="InvertDiagBlocksLowerTriangular" | custom-call | tf_op jit(solution)/shard_map/jit(cholesky)/cholesky | solution.py:102
  287.4 11.7 %cholesky.265 = f32[128,128]{1,0:T(8,128)S(1)} custom-call(f32[128,128]{1,0:T(8,128)S(1)} %convolution_subtract_fusion.7), custom_call_target="Cholesky" | custom-call | tf_op jit(solution)/shard_map/jit(cholesky)/cholesky | solution.py:102
  306.2 19.7 %custom-call.22 = f32[2,128,128]{1,2,0:T(8,128)S(1)} custom-call(f32[2,128,128]{2,1,0:T(8,128)S(1)} %get-tuple-element.31), custom_call_target="InvertDiagBlocksLowerTriangular" | custom-call | tf_op jit(solution)/shard_map/jit(_solve_triangular)/triangular_solve | solution.py:47
  328.5 47.2 %all-gather.37.cloned.1.call-done = f32[4096,256]{1,0:T(8,128)} async-done(((f32[512,256]{1,0:T(8,128)}), f32[4096,256]{1,0:T(8,128)}) %all-gather.37.cloned.1.call-update) | async-done | bytes 4194320 | tf_op jit(solution)/shard_map/all_gather | solution.py:14
  379.0 25.4 %all-gather.39.cloned.1.call-done = f32[1024,256]{1,0:T(8,128)} async-done(((f32[256,256]{1,0:T(8,128)}), f32[1024,256]{1,0:T(8,128)}) %all-gather.39.cloned.1.call-update) | async-done | bytes 1048592 | tf_op jit(solution)/shard_map/all_gather | solution.py:14
  407.3 26.7 %all-gather.41.cloned.1.call-done = f32[1024,256]{1,0:T(8,128)} async-done(((f32[256,256]{1,0:T(8,128)}), f32[1024,256]{1,0:T(8,128)}) %all-gather.41.cloned.1.call-update) | async-done | bytes 1048592 | tf_op jit(solution)/shard_map/all_gather | solution.py:14
  435.6 11.7 %cholesky.282 = f32[128,128]{1,0:T(8,128)S(1)} custom-call(f32[128,128]{1,0:T(8,128)S(1)} %cholesky.352), custom_call_target="Cholesky" | custom-call | tf_op jit(solution)/shard_map/jit(cholesky)/cholesky | solution.py:102
  447.3 9.8 %custom-call.23 = f32[1,128,128]{1,2,0:T(8,128)S(1)} custom-call(f32[1,128,128]{2,1,0:T(8,128)S(1)} %get-tuple-element.99), custom_call_target="InvertDiagBlocksLowerTriangular" | custom-call | tf_op jit(solution)/shard_map/jit(cholesky)/cholesky | solution.py:102
  457.6 11.7 %cholesky.299 = f32[128,128]{1,0:T(8,128)S(1)} custom-call(f32[128,128]{1,0:T(8,128)S(1)} %convolution_subtract_fusion.6), custom_call_target="Cholesky" | custom-call | tf_op jit(solution)/shard_map/jit(cholesky)/cholesky | solution.py:102
  476.7 19.7 %custom-call.24 = f32[2,128,128]{1,2,0:T(8,128)S(1)} custom-call(f32[2,128,128]{2,1,0:T(8,128)S(1)} %get-tuple-element.32), custom_call_target="InvertDiagBlocksLowerTriangular" | custom-call | tf_op jit(solution)/shard_map/jit(_solve_triangular)/triangular_solve | solution.py:47
  498.9 47.3 %all-gather.43.cloned.1.call-done = f32[4096,256]{1,0:T(8,128)} async-done(((f32[512,256]{1,0:T(8,128)}), f32[4096,256]{1,0:T(8,128)}) %all-gather.43.cloned.1.call-update) | async-done | bytes 4194320 | tf_op jit(solution)/shard_map/all_gather | solution.py:14
  549.5 25.4 %all-gather.45.cloned.1.call-done = f32[1024,256]{1,0:T(8,128)} async-done(((f32[256,256]{1,0:T(8,128)}), f32[1024,256]{1,0:T(8,128)}) %all-gather.45.cloned.1.call-update) | async-done | bytes 1048592 | tf_op jit(solution)/shard_map/all_gather | solution.py:14
  578.6 26.7 %all-gather.47.cloned.1.call-done = f32[1024,256]{1,0:T(8,128)} async-done(((f32[256,256]{1,0:T(8,128)}), f32[1024,256]{1,0:T(8,128)}) %all-gather.47.cloned.1.call-update) | async-done | bytes 1048592 | tf_op jit(solution)/shard_map/all_gather | solution.py:14
  606.8 11.7 %cholesky.316 = f32[128,128]{1,0:T(8,128)S(1)} custom-call(f32[128,128]{1,0:T(8,128)S(1)} %cholesky.355), custom_call_target="Cholesky" | custom-call | tf_op jit(solution)/shard_map/jit(cholesky)/cholesky | solution.py:102
  618.6 9.8 %custom-call.25 = f32[1,128,128]{1,2,0:T(8,128)S(1)} custom-call(f32[1,128,128]{2,1,0:T(8,128)S(1)} %get-tuple-element.95), custom_call_target="InvertDiagBlocksLowerTriangular" | custom-call | tf_op jit(solution)/shard_map/jit(cholesky)/cholesky | solution.py:102
  628.9 11.7 %cholesky.333 = f32[128,128]{1,0:T(8,128)S(1)} custom-call(f32[128,128]{1,0:T(8,128)S(1)} %convolution_subtract_fusion.5), custom_call_target="Cholesky" | custom-call | tf_op jit(solution)/shard_map/jit(cholesky)/cholesky | solution.py:102
  648.3 19.7 %custom-call.26 = f32[2,128,128]{1,2,0:T(8,128)S(1)} custom-call(f32[2,128,128]{2,1,0:T(8,128)S(1)} %get-tuple-element.33), custom_call_target="InvertDiagBlocksLowerTriangular" | custom-call | tf_op jit(solution)/shard_map/jit(_solve_triangular)/triangular_solve | solution.py:47
  671.6 47.2 %all-gather.49.cloned.1.call-done = f32[4096,256]{1,0:T(8,128)} async-done(((f32[512,256]{1,0:T(8,128)}), f32[4096,256]{1,0:T(8,128)}) %all-gather.49.cloned.1.call-update) | async-done | bytes 4194320 | tf_op jit(solution)/shard_map/all_gather | solution.py:14
  722.8 24.8 %all-gather.51.cloned.1.call-done = f32[1024,256]{1,0:T(8,128)} async-done(((f32[256,256]{1,0:T(8,128)}), f32[1024,256]{1,0:T(8,128)}) %all-gather.51.cloned.1.call-update) | async-done | bytes 1048592 | tf_op jit(solution)/shard_map/all_gather | solution.py:14
  (183 shorter events, 92.7 us)
Async XLA Ops:
  9.2 9.0 %copy-start.2 = (s32[8,1]{0,1:T(1,128)S(1)}, s32[8,1]{0,1:T(1,128)}, u32[]{:S(2)}) copy-start(s32[8,1]{0,1:T(1,128)} %param.10) | copy-start | bytes 100
  9.2 9.0 %copy-start.3 = (s32[8,1]{0,1:T(1,128)S(1)}, s32[8,1]{0,1:T(1,128)}, u32[]{:S(2)}) copy-start(s32[8,1]{0,1:T(1,128)} %param.9) | copy-start | bytes 100
  11.8 21.7 %all-to-all-start = ((bf16[8,64,440]{2,1,0:T(8,128)(2,1)}), bf16[8,64,440]{2,1,0:T(8,128)(2,1)S(1)}, u32[]{:S(2)}, u32[]{:S(2)}) async-start(bf16[8,64,440]{2,1,0:T(8,128)(2,1)} %bitcast.1), calls=%async_computation | async-start | bytes 1048576 | tf_op jit(solution)/shard_map/all_to_all | solution.py:69
  18.1 45.4 %all-gather.27.cloned.1.call-start = ((), (), s32[]{:S(2)}) async-start(), calls=%async_computation.1 | async-start | bytes 2359296 | tf_op jit(solution)/shard_map/all_gather | solution.py:83
  35.3 30.6 %copy-start = (bf16[256,440]{1,0:T(8,128)(2,1)S(1)}, bf16[256,440]{1,0:T(8,128)(2,1)}, u32[]{:S(2)}) copy-start(bf16[256,440]{1,0:T(8,128)(2,1)} %gather_fusion.1) | copy-start | bytes 675844
  35.4 58.2 %all-gather.29.cloned.1.call-start = ((), (), s32[]{:S(2)}) async-start(), calls=%async_computation.2 | async-start | bytes 1310720 | tf_op jit(solution)/shard_map/all_gather | solution.py:14
  67.3 138.1 %all-gather.31.cloned.1.call-start = ((), (), s32[]{:S(2)}) async-start(), calls=%async_computation.3 | async-start | bytes 4718592 | tf_op jit(solution)/shard_map/all_gather | solution.py:14
  158.0 76.1 %all-gather.33.cloned.1.call-start = ((), (), s32[]{:S(2)}) async-start(), calls=%async_computation.4 | async-start | bytes 1310720 | tf_op jit(solution)/shard_map/all_gather | solution.py:14
  208.6 55.2 %all-gather.35.cloned.1.call-start = ((), (), s32[]{:S(2)}) async-start(), calls=%async_computation.5 | async-start | bytes 1310720 | tf_op jit(solution)/shard_map/all_gather | solution.py:14
  237.0 138.7 %all-gather.37.cloned.1.call-start = ((), (), s32[]{:S(2)}) async-start(), calls=%async_computation.6 | async-start | bytes 4718592 | tf_op jit(solution)/shard_map/all_gather | solution.py:14
  328.4 76.1 %all-gather.39.cloned.1.call-start = ((), (), s32[]{:S(2)}) async-start(), calls=%async_computation.7 | async-start | bytes 1310720 | tf_op jit(solution)/shard_map/all_gather | solution.py:14
  379.0 55.0 %all-gather.41.cloned.1.call-start = ((), (), s32[]{:S(2)}) async-start(), calls=%async_computation.8 | async-start | bytes 1310720 | tf_op jit(solution)/shard_map/all_gather | solution.py:14
  407.3 138.9 %all-gather.43.cloned.1.call-start = ((), (), s32[]{:S(2)}) async-start(), calls=%async_computation.9 | async-start | bytes 4718592 | tf_op jit(solution)/shard_map/all_gather | solution.py:14
  498.9 76.1 %all-gather.45.cloned.1.call-start = ((), (), s32[]{:S(2)}) async-start(), calls=%async_computation.10 | async-start | bytes 1310720 | tf_op jit(solution)/shard_map/all_gather | solution.py:14
  549.5 55.8 %all-gather.47.cloned.1.call-start = ((), (), s32[]{:S(2)}) async-start(), calls=%async_computation.11 | async-start | bytes 1310720 | tf_op jit(solution)/shard_map/all_gather | solution.py:14
  578.5 140.3 %all-gather.49.cloned.1.call-start = ((), (), s32[]{:S(2)}) async-start(), calls=%async_computation.12 | async-start | bytes 4718592 | tf_op jit(solution)/shard_map/all_gather | solution.py:14
  606.6 61.4 %copy-start.1 = (f32[256,512]{0,1:T(8,128)S(1)}, f32[256,512]{0,1:T(8,128)}, u32[]{:S(2)}) copy-start(f32[256,512]{0,1:T(8,128)} %get-tuple-element.120) | copy-start | bytes 1572868
  671.5 76.1 %all-gather.51.cloned.1.call-start = ((), (), s32[]{:S(2)}) async-start(), calls=%async_computation.13 | async-start | bytes 1310720 | tf_op jit(solution)/shard_map/all_gather | solution.py:14
Sparse Core Ops, SparseCore 0:
  35.5 27.9 all-gather.26
  67.4 26.1 all-gather.28
  158.1 47.1 all-gather.30
  208.7 25.3 all-gather.32
  237.1 26.6 all-gather.34
  328.5 47.1 all-gather.36
  379.1 25.3 all-gather.38
  407.4 26.6 all-gather.40
  499.0 47.1 all-gather.42
  549.6 25.3 all-gather.44
  578.6 26.6 all-gather.46
  671.7 47.1 all-gather.48
  722.2 25.3 all-gather.50
